TPU v7x, 512 devices: a whole 4x8x8 slice. The times are simulated.
512 devices in a mesh: band: 32 (over x, y), seq: 16 (over z, core).
Axes of the slice: x: 4, y: 8, z: 8, core: 2. Of those that a mesh axis runs over, the one named last changes fastest.
Arguments:
- posteriors: bfloat16 [32, 262144], P(None, ('band', 'seq'))
- seed_mask: int32 [262144], P(('band', 'seq')), may hold values 0 or 1
- frame_perm: int32 [512, 512], P(('band', 'seq')), may hold values from 0 to 511, each once within a row
- lengths: int32 [256], replicated, may hold values from 1 to 4096, 262144 in all
- embeddings: bfloat16 [262144, 256], P(('band', 'seq')), may hold values from -12 to 12
- partners: int32 [2048, 32], P(('band', 'seq')), may hold values from 0 to 127, as said below
- levels: int32 [2048, 32], P(('band', 'seq')), may hold values from 1 to 8, as said below
Outputs:
- spread_labels: float32 [32, 262144], P(None, ('band', 'seq'))
Inputs may be any that keep to these rules, and one draw needn't show every extreme that they name: `partners`: within each seq index s, slot k pairs the 128 tiles mutually: if tile number a names b in slot k then b names a in slot k; no tile names itself. `levels`: two tiles paired in slot k carry the same level.
All inputs are finite; a program needn't handle non-finite values. No bound on the sum of `seed_mask` on one device may be relied on, other than what follows from the above.
Results may differ from a plain program's by a relative error of at most 0.007.
Values may be sent and summed in bfloat16 or wider, within the bound.
No kernel may reach another device: no remote copies, remote signals or barrier semaphores. Data moves between devices by JAX's collectives and lax.ppermute only.
A program may use at most 64 MiB of HBM per device.

v0:
```python
import math
import jax
import jax.numpy as jnp
from jax import lax
from jax.sharding import PartitionSpec as P

RADIUS = 64
ITERS = 3
decay_len = 16.0
spread_rate = 0.9


def with_halo(cells, sides, width):
    for axis, dim in sides:
        count = lax.axis_size(axis)
        ends = count - 1
        head = lax.slice_in_dim(cells, 0, width, axis=dim)
        tail = lax.slice_in_dim(cells, cells.shape[dim] - width, cells.shape[dim], axis=dim)
        cells = jnp.concatenate(
            [
                lax.ppermute(tail, axis, [(i, (i + 1) % count) for i in range(ends)]),
                cells,
                lax.ppermute(head, axis, [((i + 1) % count, i) for i in range(ends)]),
            ],
            axis=dim,
        )
    return cells


def on_device(posteriors, seed_mask, frame_perm, lengths, embeddings, partners, levels):
    channels, frames = posteriors.shape
    band_count = lax.axis_size("band")
    groups = lax.axis_size("seq")
    tile_count = frames // 128
    seeded = posteriors * seed_mask.astype(jnp.bfloat16)[None, :]
    ordered = jnp.take(seeded, frame_perm[0], axis=1).reshape(
        channels, band_count, frames // band_count
    )
    arrived = lax.all_to_all(ordered, "band", split_axis=1, concat_axis=1, tiled=True)
    labels = arrived.reshape(channels, frames).astype(jnp.float32)
    device = lax.axis_index("band") * groups + lax.axis_index("seq")
    frame_total = frames * band_count * groups
    window = 128 + 2 * RADIUS
    global_at = device * frames - RADIUS + jnp.arange(frames + 2 * RADIUS, dtype=jnp.int32)
    utt_ends = jnp.cumsum(lengths)
    owner_seg = jnp.sum((utt_ends[None, :] <= global_at[:, None]).astype(jnp.int32), axis=1)
    inside = (global_at >= 0) & (global_at < frame_total)
    tile_off = (jnp.arange(tile_count, dtype=jnp.int32) * 128)[:, None, None]
    win_pos = tile_off + jnp.arange(window, dtype=jnp.int32)[None, :, None]
    row_pos = tile_off + RADIUS + jnp.arange(128, dtype=jnp.int32)[None, None, :]
    offset = jnp.abs(win_pos - row_pos)
    linked = (
        (offset >= 1)
        & (offset <= RADIUS)
        & (owner_seg[win_pos] == owner_seg[row_pos])
        & inside[win_pos]
    )
    band_tiles = jnp.where(
        linked, jnp.exp(-offset.astype(jnp.float32) / decay_len), jnp.float32(0.0)
    ).astype(jnp.bfloat16)
    near_degree = jnp.sum(band_tiles.astype(jnp.float32), axis=1).reshape(frames)
    gathered = lax.all_gather(embeddings, "band", axis=0, tiled=True)
    embed_width = embeddings.shape[1]
    partner_rows = gathered.reshape(-1, 128, embed_width)[partners]
    own_rows = embeddings.reshape(tile_count, 128, embed_width)
    inner_prod = jnp.einsum(
        "tkje,tie->tkji", partner_rows, own_rows, preferred_element_type=jnp.float32
    )
    affinity = (
        jnp.exp(0.5 * (inner_prod / math.sqrt(embed_width)))
        * (levels.astype(jnp.float32) / 8.0)[:, :, None, None]
        / 128.0
    )
    affinity = affinity.astype(jnp.bfloat16)
    far_degree = jnp.sum(affinity.astype(jnp.float32), axis=(1, 2)).reshape(frames)
    norm_scale = 1.0 / jnp.sqrt(near_degree + far_degree)

    def squares(residual):
        return lax.psum(jnp.sum(residual * residual, axis=1), ("band", "seq"))

    solution = jnp.zeros((channels, frames), jnp.float32)
    residual = labels
    direction = labels
    norm_now = squares(residual)
    for iteration in range(ITERS):
        lifted = (norm_scale[None, :] * direction).astype(jnp.bfloat16)
        padded = with_halo(lifted, ((("band", "seq"), 1),), RADIUS)
        windows = jnp.stack(
            [padded[:, position * 128 : position * 128 + window] for position in range(tile_count)],
            axis=0,
        )
        near_term = jnp.einsum(
            "tcw,twa->cta", windows, band_tiles, preferred_element_type=jnp.float32
        ).reshape(channels, frames)
        spread = lax.all_gather(lifted, "band", axis=1, tiled=True).reshape(channels, -1, 128)
        far_tiles = spread[:, partners]
        far_term = jnp.einsum(
            "ctkj,tkji->cti", far_tiles, affinity, preferred_element_type=jnp.float32
        ).reshape(channels, frames)
        image = direction - spread_rate * norm_scale[None, :] * (near_term + far_term)
        curve = lax.psum(jnp.sum(direction * image, axis=1), ("band", "seq"))
        alpha = norm_now / curve
        solution = solution + alpha[:, None] * direction
        residual = residual - alpha[:, None] * image
        norm_next = squares(residual)
        direction = residual + (norm_next / norm_now)[:, None] * direction
        norm_now = norm_next
    return solution


def solution(mesh):
    placed = (
        P(None, ("band", "seq")),
        P(("band", "seq")),
        P(("band", "seq"), None),
        P(),
        P(("band", "seq"), None),
        P(("band", "seq"), None),
        P(("band", "seq"), None),
    )
    return jax.shard_map(
        on_device, mesh=mesh, in_specs=placed, out_specs=P(None, ("band", "seq")), check_vma=False
    )
```

profile of v0, /device:TPU:1, one launch (start us, length us, event | category | flops | bytes accessed | tf_op | source)
XLA Modules:
  0.0 862.8 jit_solution(14141777168958132764)
XLA Ops:
  6.5 0.7 all-gather.5.cloned.1.call-update
  7.3 0.7 convert_element_type.47
  7.9 0.8 broadcast_multiply_fusion
  8.8 0.5 broadcast.328
  9.4 1.3 reduce.11
  10.8 0.7 compare_select_fusion.1
  11.5 1.3 gather_fusion
  12.8 0.1 fusion.73
  13.0 0.8 reshape.489
  13.7 10.5 %all-to-all-start = ((bf16[32,2,256]{2,1,0:T(2,128)(2,1)}), bf16[32,2,256]{2,1,0:T(2,128)(2,1)S(1)}, u32[]{:S(2)}, u32[]{:S(2)}) async-start(bf16[32,2,256]{2,1,0:T(2,128)(2,1)} %reshape.489), calls=%async_computation | async-start | bytes 65536 | tf_op jit(solution)/shard_map/all_to_all | solution.py:39
  24.3 1.0 reduce-window.9
  25.7 0.3 convert_reduce_fusion.1
  26.0 4.5 gather_fusion.1
  30.6 2.3 gather_fusion.2
  32.9 6.8 gather_fusion.3
  40.0 0.6 convert_reduce_fusion.2
  40.8 78.1 %all-gather.5.cloned.1.call-done = bf16[16384,256]{1,0:T(8,128)(2,1)} async-done(((bf16[512,256]{1,0:T(8,128)(2,1)}), bf16[16384,256]{1,0:T(8,128)(2,1)}) %all-gather.5.cloned.1.call-update) | async-done | bytes 8388624 | tf_op jit(solution)/shard_map/all_gather | solution.py:62
  118.9 10.0 %gather_fusion.4 = bf16[128,128,256]{2,1,0:T(8,128)(2,1)} fusion(bf16[128,128,256]{2,1,0:T(8,128)(2,1)} %bitcast.161, s32[1024]{0:T(1024)S(1)} %pad_clamp_fusion), kind=kCustom, calls=%fused_computation.4 | custom fusion | bytes 16777728 | tf_op jit(solution)/shard_map/gather | solution.py:64
  128.9 7.7 convert_reduce_fusion
  136.6 0.6 multiply_convert_fusion.3
  137.3 0.8 fusion.72
  138.1 4.2 collective-permute-start
  142.4 1.9 collective-permute-start.1
  144.4 2.9 collective-permute-done.1
  147.3 0.9 fusion.49
  148.3 0.6 fusion.13
  148.9 58.6 %all-gather.7.cloned.1.call-done = bf16[32,16384]{1,0:T(8,128)(2,1)} async-done(((bf16[32,512]{1,0:T(8,128)(2,1)}), bf16[32,16384]{1,0:T(8,128)(2,1)}) %all-gather.7.cloned.1.call-update) | async-done | bytes 1048592 | tf_op jit(solution)/shard_map/all_gather | solution.py:95
  207.5 1.4 copy_bitcast_fusion.2
  208.9 0.8 gather_fusion.5
  209.7 2.9 fusion.3
  212.8 0.2 fusion.10
  212.9 102.0 %all-reduce = (f32[32]{0:T(128)S(1)}, f32[32]{0:T(128)S(1)}) all-reduce(f32[32]{0:T(128)S(1)} %get-tuple-element.6, f32[32]{0:T(128)S(1)} %get-tuple-element.5), channel_id=1, replica_groups=mesh['band'=32,'seq'=16] {'band','seq'}, use_global_device_ids=true, to_apply=%region_1.2 | all-reduce | flops 64 | bytes 512 | tf_op jit(solution)/shard_map/psum | solution.py:79
  315.0 0.2 multiply_reduce_fusion.2
  315.1 94.4 %psum.44 = f32[32]{0:T(128)S(1)} all-reduce(f32[32]{0:T(128)S(1)} %multiply_reduce_fusion.2), channel_id=1, replica_groups=mesh['band'=32,'seq'=16] {'band','seq'}, use_global_device_ids=true, to_apply=%region_10.11 | all-reduce | flops 32 | bytes 256 | tf_op jit(solution)/shard_map/psum | solution.py:79
  409.5 0.7 multiply_convert_fusion.2
  410.3 0.8 fusion.71
  411.1 3.1 collective-permute-start.2
  414.2 2.1 collective-permute-start.3
  416.3 2.9 collective-permute-done.3
  419.1 0.9 fusion.47
  420.1 0.6 fusion.14
  420.7 57.0 %all-gather.9.cloned.1.call-done = bf16[32,16384]{1,0:T(8,128)(2,1)} async-done(((bf16[32,512]{1,0:T(8,128)(2,1)}), bf16[32,16384]{1,0:T(8,128)(2,1)}) %all-gather.9.cloned.1.call-update) | async-done | bytes 1048592 | tf_op jit(solution)/shard_map/all_gather | solution.py:95
  477.7 1.4 copy_bitcast_fusion.1
  479.1 0.8 gather_fusion.6
  479.9 2.9 fusion.2
  482.8 0.1 copy.53
  482.9 0.2 multiply_reduce_fusion.1
  483.1 102.0 %psum.45 = f32[32]{0:T(128)S(1)} all-reduce(f32[32]{0:T(128)S(1)} %multiply_reduce_fusion.1), channel_id=1, replica_groups=mesh['band'=32,'seq'=16] {'band','seq'}, use_global_device_ids=true, to_apply=%region_12.13 | all-reduce | flops 32 | bytes 256 | tf_op jit(solution)/shard_map/psum | solution.py:101
  585.2 0.2 multiply_reduce_fusion
  585.4 94.4 %psum.46 = f32[32]{0:T(128)S(1)} all-reduce(f32[32]{0:T(128)S(1)} %multiply_reduce_fusion), channel_id=1, replica_groups=mesh['band'=32,'seq'=16] {'band','seq'}, use_global_device_ids=true, to_apply=%region_14.15 | all-reduce | flops 32 | bytes 256 | tf_op jit(solution)/shard_map/psum | solution.py:79
  679.8 0.7 multiply_convert_fusion.1
  680.5 0.8 fusion.70
  681.3 3.1 collective-permute-start.4
  684.4 1.9 collective-permute-start.5
  686.3 3.0 collective-permute-done.5
  689.3 0.9 fusion.45
  690.3 0.6 fusion.15
  690.9 57.1 %all-gather.11.cloned.1.call-done = bf16[32,16384]{1,0:T(8,128)(2,1)} async-done(((bf16[32,512]{1,0:T(8,128)(2,1)}), bf16[32,16384]{1,0:T(8,128)(2,1)}) %all-gather.11.cloned.1.call-update) | async-done | bytes 1048592 | tf_op jit(solution)/shard_map/all_gather | solution.py:95
  748.0 1.4 copy_bitcast_fusion
  749.4 0.8 gather_fusion.7
  750.1 2.9 fusion.1
  753.2 0.2 fusion.12
  753.5 102.0 %psum.47 = f32[32]{0:T(128)S(1)} all-reduce(f32[32]{0:T(128)S(1)} %fusion.12), channel_id=1, replica_groups=mesh['band'=32,'seq'=16] {'band','seq'}, use_global_device_ids=true, to_apply=%region_16.17 | all-reduce | flops 32 | bytes 256 | tf_op jit(solution)/shard_map/psum | solution.py:101
  855.5 0.7 multiply_add_fusion
  (54 shorter events, 1.7 us)
Async XLA Ops:
  6.5 33.2 %copy-start.1 = (s32[4,32]{1,0:T(4,128)S(1)}, s32[4,32]{1,0:T(4,128)}, u32[]{:S(2)}) copy-start(s32[4,32]{1,0:T(4,128)} %param.12) | copy-start | bytes 1540
  6.5 34.0 %copy-start.2 = (s32[4,32]{1,0:T(4,128)S(1)}, s32[4,32]{1,0:T(4,128)}, u32[]{:S(2)}) copy-start(s32[4,32]{1,0:T(4,128)} %param.13) | copy-start | bytes 1540
  6.5 112.4 %all-gather.5.cloned.1.call-start = ((), (), s32[]{:S(2)}) async-start(), calls=%async_computation.1 | async-start | bytes 8650752 | tf_op jit(solution)/shard_map/all_gather | solution.py:62
  13.7 26.9 %all-to-all-start = ((bf16[32,2,256]{2,1,0:T(2,128)(2,1)}), bf16[32,2,256]{2,1,0:T(2,128)(2,1)S(1)}, u32[]{:S(2)}, u32[]{:S(2)}) async-start(bf16[32,2,256]{2,1,0:T(2,128)(2,1)} %reshape.489), calls=%async_computation | async-start | bytes 65536 | tf_op jit(solution)/shard_map/all_to_all | solution.py:39
  24.3 183.2 %all-gather.7.cloned.1.call-start = ((), (), s32[]{:S(2)}) async-start(), calls=%async_computation.2 | async-start | bytes 1081344 | tf_op jit(solution)/shard_map/all_gather | solution.py:95
  118.9 10.0 %copy-start = (bf16[512,256]{1,0:T(8,128)(2,1)S(1)}, bf16[512,256]{1,0:T(8,128)(2,1)}, u32[]{:S(2)}) copy-start(bf16[512,256]{1,0:T(8,128)(2,1)} %param.11) | copy-start | bytes 786436
  137.3 340.4 %all-gather.9.cloned.1.call-start = ((), (), s32[]{:S(2)}) async-start(), calls=%async_computation.3 | async-start | bytes 1081344 | tf_op jit(solution)/shard_map/all_gather | solution.py:95
  138.1 6.3 collective-permute-start
  142.4 5.0 collective-permute-start.1
  410.2 337.7 %all-gather.11.cloned.1.call-start = ((), (), s32[]{:S(2)}) async-start(), calls=%async_computation.4 | async-start | bytes 1081344 | tf_op jit(solution)/shard_map/all_gather | solution.py:95
  411.1 5.2 collective-permute-start.2
  414.2 5.0 collective-permute-start.3
  681.3 5.0 collective-permute-start.4
  684.4 5.0 collective-permute-start.5
Sparse Core Ops, SparseCore 0:
  10.5 108.3 all-gather.4
  137.4 70.0 all-gather.6
  410.4 67.2 all-gather.8
  680.6 67.2 all-gather.10
where the time goes:
time: 864 us; the launch traced here: 863 us
  blocking collectives  495 us (57%)
  waiting for transfers between devices  260 us (30%)
  local copies, waits for them, and re-layouts  36.3 us (4%)
  starting transfers between devices  26.9 us (3%)
  matrix products  18.3 us (2%)
  between operations  13.5 us (2%)
  other arithmetic  12.5 us (1%)
    psum x3, blocking collectives, squares(): return lax.psum(jnp.sum(residual * residual, axis=1), ('band', 'seq'))  291 us
    psum x2, blocking collectives, on_device(): curve = lax.psum(jnp.sum(direction * image, axis=1), ('band', 'seq'))  204 us
    all_gather x3, waiting for transfers between devices, on_device(): lax.all_gather(lifted, 'band', axis=1, tiled=True)  173 us
    all_gather x1, waiting for transfers between devices, on_device(): gathered = lax.all_gather(embeddings, 'band', axis=0, tiled=True)  78.1 us
  transfers between devices with their start and end apart: 11, of which 7 were waited for; matrix products, arithmetic and copies ran while one was open for 3% of the time, Pallas kernels for 0%

commit v1 on v0

--- a/solution.py
+++ b/solution.py
@@ -76,7 +76,12 @@
     norm_scale = 1.0 / jnp.sqrt(near_degree + far_degree)
 
     def squares(residual):
-        return lax.psum(jnp.sum(residual * residual, axis=1), ("band", "seq"))
+
+        def serve_arrays(q_in):
+            outer = lax.all_gather(q_in, ("band", "seq")).sum(axis=0)
+            return outer
+
+        return serve_arrays(jnp.sum(residual * residual, axis=1))
 
     solution = jnp.zeros((channels, frames), jnp.float32)
     residual = labels

time: 864 us -> 1350 us (1.56)
  waiting for transfers between devices: 260 us -> 925 us
  blocking collectives: 495 us -> 307 us
    unnamed x4 -> x10, waiting for transfers between devices: 0.76 us -> 669 us
    psum x3 -> x0, blocking collectives: 291 us -> none  [squares(): return lax.psum(jnp.sum(residual * residual, axis=1), ('band', 'seq'))]
    psum x2 -> x3, blocking collectives: 204 us -> 307 us  [on_device(): curve = lax.psum(jnp.sum(direction * image, axis=1), ('band', 'seq'))]
  transfers between devices with their start and end apart: 11 -> 14, of which waited for: 7 -> 10; matrix products, arithmetic and copies ran while one was open for 3% -> 2% of each run, Pallas kernels for 0% -> 0%
where the time goes in v1:
time: 1350 us
  waiting for transfers between devices  925 us (69%)
  blocking collectives  307 us (23%)
  local copies, waits for them, and re-layouts  41.9 us (3%)
  starting transfers between devices  27.1 us (2%)
  matrix products  18.3 us (1%)
  between operations  13.9 us (1%)
    unnamed x10, waiting for transfers between devices  669 us
    psum x3, blocking collectives, on_device(): curve = lax.psum(jnp.sum(direction * image, axis=1), ('band', 'seq'))  307 us
    all_gather x3, waiting for transfers between devices, on_device(): lax.all_gather(lifted, 'band', axis=1, tiled=True)  168 us
    all_gather x1, waiting for transfers between devices, on_device(): gathered = lax.all_gather(embeddings, 'band', axis=0, tiled=True)  78.1 us
  transfers between devices with their start and end apart: 14, of which 10 were waited for; matrix products, arithmetic and copies ran while one was open for 2% of the time, Pallas kernels for 0%

profile of v1, /device:TPU:1, one launch (start us, length us, event | category | flops | bytes accessed | tf_op | source)
XLA Modules:
  0.0 1345.9 jit_solution(7462095712962470974)
XLA Ops:
  6.5 0.7 all-gather.8.cloned.1.call-update
  7.3 0.7 convert_element_type.47
  7.9 0.8 broadcast_multiply_fusion
  8.8 0.5 broadcast.327
  9.4 1.3 reduce.11
  10.8 0.7 compare_select_fusion.1
  11.5 1.3 gather_fusion
  13.0 0.8 reshape.508
  13.7 10.5 all-to-all-start
  24.3 1.0 reduce-window.9
  26.0 4.5 gather_fusion.1
  30.6 2.3 gather_fusion.2
  32.9 6.8 gather_fusion.3
  40.0 0.6 convert_reduce_fusion.2
  40.8 78.1 %all-gather.8.cloned.1.call-done = bf16[16384,256]{1,0:T(8,128)(2,1)} async-done(((bf16[512,256]{1,0:T(8,128)(2,1)}), bf16[16384,256]{1,0:T(8,128)(2,1)}) %all-gather.8.cloned.1.call-update) | async-done | bytes 8388624 | tf_op jit(solution)/shard_map/all_gather | solution.py:62
  118.9 10.0 gather_fusion.4
  128.9 7.7 convert_reduce_fusion
  136.6 0.6 multiply_convert_fusion.3
  137.3 0.8 fusion.72
  138.1 4.2 collective-permute-start
  142.4 1.9 collective-permute-start.1
  144.4 2.9 collective-permute-done.1
  147.3 0.9 fusion.49
  148.3 0.6 fusion.13
  148.9 58.6 %all-gather.10.cloned.1.call-done = bf16[32,16384]{1,0:T(8,128)(2,1)} async-done(((bf16[32,512]{1,0:T(8,128)(2,1)}), bf16[32,16384]{1,0:T(8,128)(2,1)}) %all-gather.10.cloned.1.call-update) | async-done | bytes 1048592 | tf_op jit(solution)/shard_map/all_gather | solution.py:100
  207.5 1.4 copy_bitcast_fusion.2
  208.9 0.8 gather_fusion.5
  209.7 2.9 fusion.3
  212.9 0.3 dynamic-update-slice
  213.2 0.6 copy-done.2
  213.9 103.2 %psum.21 = f32[32]{0:T(128)S(1)} all-reduce(f32[32]{0:T(128)S(1)} %get-tuple-element.5), channel_id=1, replica_groups=mesh['band'=32,'seq'=16] {'band','seq'}, use_global_device_ids=true, to_apply=%region_8.9 | all-reduce | flops 32 | bytes 256 | tf_op jit(solution)/shard_map/psum | solution.py:106
  317.0 159.8 %all-reduce.7.cloned.1.call-done = f32[16384]{0:T(1024)} async-done(((f32[16384]{0:T(1024)}), f32[16384]{0:T(1024)}) %all-reduce.7.cloned.1.call-update) | async-done | bytes 65552
  476.9 0.9 reshape.468
  478.4 0.6 copy-done.3
  479.1 254.7 %all-reduce.9.cloned.1.call-done = f32[16384]{0:T(1024)} async-done(((f32[16384]{0:T(1024)}), f32[16384]{0:T(1024)}) %all-reduce.9.cloned.1.call-update) | async-done | bytes 65552
  733.7 0.9 reshape.469
  734.8 0.7 multiply_convert_fusion.2
  735.6 0.8 fusion.71
  736.3 3.1 collective-permute-start.2
  739.4 2.1 collective-permute-start.3
  741.6 2.9 collective-permute-done.3
  744.4 0.9 fusion.47
  745.4 0.6 fusion.14
  745.9 54.6 %all-gather.12.cloned.1.call-done = bf16[32,16384]{1,0:T(8,128)(2,1)} async-done(((bf16[32,512]{1,0:T(8,128)(2,1)}), bf16[32,16384]{1,0:T(8,128)(2,1)}) %all-gather.12.cloned.1.call-update) | async-done | bytes 1048592 | tf_op jit(solution)/shard_map/all_gather | solution.py:100
  800.5 1.4 copy_bitcast_fusion.1
  801.9 0.8 gather_fusion.6
  802.7 2.9 fusion.2
  806.0 102.0 %psum.22 = f32[32]{0:T(128)S(1)} all-reduce(f32[32]{0:T(128)S(1)} %multiply_reduce_fusion.1), channel_id=1, replica_groups=mesh['band'=32,'seq'=16] {'band','seq'}, use_global_device_ids=true, to_apply=%region_12.13 | all-reduce | flops 32 | bytes 256 | tf_op jit(solution)/shard_map/psum | solution.py:106
  908.5 0.6 copy-done.1
  909.2 254.1 %all-reduce.11.cloned.1.call-done = f32[16384]{0:T(1024)} async-done(((f32[16384]{0:T(1024)}), f32[16384]{0:T(1024)}) %all-reduce.11.cloned.1.call-update) | async-done | bytes 65552
  1163.3 0.9 reshape.470
  1164.4 0.7 multiply_convert_fusion.1
  1165.1 0.8 fusion.70
  1165.9 3.1 collective-permute-start.4
  1169.0 1.9 collective-permute-start.5
  1171.0 3.0 collective-permute-done.5
  1174.0 0.9 fusion.45
  1174.9 0.6 fusion.15
  1175.5 55.2 %all-gather.14.cloned.1.call-done = bf16[32,16384]{1,0:T(8,128)(2,1)} async-done(((bf16[32,512]{1,0:T(8,128)(2,1)}), bf16[32,16384]{1,0:T(8,128)(2,1)}) %all-gather.14.cloned.1.call-update) | async-done | bytes 1048592 | tf_op jit(solution)/shard_map/all_gather | solution.py:100
  1230.7 1.4 copy_bitcast_fusion
  1232.2 0.8 gather_fusion.7
  1232.9 2.9 fusion.1
  1236.2 102.0 %psum.23 = f32[32]{0:T(128)S(1)} all-reduce(f32[32]{0:T(128)S(1)} %fusion.12), channel_id=1, replica_groups=mesh['band'=32,'seq'=16] {'band','seq'}, use_global_device_ids=true, to_apply=%region_16.17 | all-reduce | flops 32 | bytes 256 | tf_op jit(solution)/shard_map/psum | solution.py:106
  1338.3 0.7 multiply_add_fusion
  (79 shorter events, 4.2 us)
Async XLA Ops:
  6.5 33.2 %copy-start.4 = (s32[4,32]{1,0:T(4,128)S(1)}, s32[4,32]{1,0:T(4,128)}, u32[]{:S(2)}) copy-start(s32[4,32]{1,0:T(4,128)} %param.12) | copy-start | bytes 1540
  6.5 34.0 %copy-start.5 = (s32[4,32]{1,0:T(4,128)S(1)}, s32[4,32]{1,0:T(4,128)}, u32[]{:S(2)}) copy-start(s32[4,32]{1,0:T(4,128)} %param.13) | copy-start | bytes 1540
  6.5 112.4 %all-gather.8.cloned.1.call-start = ((), (), s32[]{:S(2)}) async-start(), calls=%async_computation.1 | async-start | bytes 8650752 | tf_op jit(solution)/shard_map/all_gather | solution.py:62
  13.7 26.8 %all-to-all-start = ((bf16[32,2,256]{2,1,0:T(2,128)(2,1)}), bf16[32,2,256]{2,1,0:T(2,128)(2,1)S(1)}, u32[]{:S(2)}, u32[]{:S(2)}) async-start(bf16[32,2,256]{2,1,0:T(2,128)(2,1)} %reshape.508), calls=%async_computation | async-start | bytes 65536 | tf_op jit(solution)/shard_map/all_to_all | solution.py:39
  24.3 183.2 %all-gather.10.cloned.1.call-start = ((), (), s32[]{:S(2)}) async-start(), calls=%async_computation.2 | async-start | bytes 1081344 | tf_op jit(solution)/shard_map/all_gather | solution.py:100
  118.9 10.0 copy-start
  137.3 339.6 %all-reduce.7.cloned.1.call-start = ((), (), s32[]{:S(2)}) async-start(), calls=%async_computation.5 | async-start | bytes 131072
  138.1 6.3 collective-permute-start
  142.4 5.0 collective-permute-start.1
  213.2 0.6 copy-start.2
  213.8 519.9 %all-reduce.9.cloned.1.call-start = ((), (), s32[]{:S(2)}) async-start(), calls=%async_computation.6 | async-start | bytes 131072
  478.4 0.6 copy-start.3
  479.0 321.5 %all-gather.12.cloned.1.call-start = ((), (), s32[]{:S(2)}) async-start(), calls=%async_computation.3 | async-start | bytes 1081344 | tf_op jit(solution)/shard_map/all_gather | solution.py:100
  735.5 427.8 %all-reduce.11.cloned.1.call-start = ((), (), s32[]{:S(2)}) async-start(), calls=%async_computation.7 | async-start | bytes 131072
  736.3 5.2 collective-permute-start.2
  739.4 5.0 collective-permute-start.3
  908.5 0.6 copy-start.1
  909.2 321.6 %all-gather.14.cloned.1.call-start = ((), (), s32[]{:S(2)}) async-start(), calls=%async_computation.4 | async-start | bytes 1081344 | tf_op jit(solution)/shard_map/all_gather | solution.py:100
  1165.9 5.0 collective-permute-start.4
  1169.0 5.0 collective-permute-start.5
Sparse Core Ops, SparseCore 0:
  10.5 108.3 all-gather.7
  137.4 70.0 all-gather.9
  214.0 262.8 all-reduce.6
  482.5 251.2 all-reduce.8
  736.6 63.8 all-gather.11
  909.3 254.0 all-reduce.10
  1166.8 63.8 all-gather.13
